TPU v7x, 128 devices: a whole 4x4x4 slice. The times are simulated.
128 devices in a mesh: pipe: 8 (over z, core), ctx: 16 (over y, x).
Axes of the slice: x: 4, y: 4, z: 4, core: 2. Of those that a mesh axis runs over, the one named last changes fastest.
Arguments:
- grad_in: bfloat16 [8, 4096, 8192], P('pipe', 'ctx'), may hold values from -6 to 6
- query: bfloat16 [8, 4096, 512], P('pipe', 'ctx'), may hold values from -8 to 8
- keyval: bfloat16 [8, 4096, 256], P('pipe', 'ctx'), may hold values from -8 to 8
- w_qkv: bfloat16 [8, 8192, 768], P('pipe', 'ctx'), may hold values from -0.0625 to 0.0625
- w_out: bfloat16 [8, 8192, 512], P('pipe', 'ctx'), may hold values from -0.25 to 0.25
- doc_lengths: int32 [8, 8], P('pipe'), may hold values from 1 to 2048, 4096 in all within a row
- order: int32 [8, 32], P('pipe'), may hold values from 0 to 31, as said below
Outputs:
- passed_grad: bfloat16 [8, 4096, 8192], P('pipe', 'ctx')
Inputs may be any that keep to these rules, and one draw needn't show every extreme that they name: Each row of order is a permutation of 0 to 31; entry d * 2 + k (device d's stored slot k, k < 2) names one of the sequence blocks e * 2 to e * 2 + 1 of device e = (d + k * 8) mod 16. `doc_lengths`: each row sums to 4096 and its largest entry is 2048.
All inputs are finite; a program needn't handle non-finite values.
Results may differ from a plain program's by a relative error of at most 0.015.
Values may be sent and summed in bfloat16 or wider, within the bound.
No kernel may reach another device: no remote copies, remote signals or barrier semaphores. Data moves between devices by JAX's collectives and lax.ppermute only.
A program may use at most 128 MiB of HBM per device.

v0:
```python
import math
import jax
import jax.numpy as jnp
from jax import lax
from jax.sharding import PartitionSpec as P

BLOCK = 128
ROPE_BASE = 500000.0
MASKED = -1e30


def passed_along(value, axis, steps):
    count = lax.axis_size(axis)
    pairs = [(source, (source + steps) % count) for source in range(count)]
    return lax.ppermute(value, axis, pairs)


def passed_along_2(value, axis, by):
    size = lax.axis_size(axis)
    pairs = [(i, i + by) for i in range(size) if 0 <= i + by < size]
    return lax.ppermute(value, axis, pairs)


def rope_tables(positions, head_dim):
    half_width = head_dim // 2
    inv_freq = ROPE_BASE ** (-(jnp.arange(half_width, dtype=jnp.float32) * 2.0 / head_dim))
    angles = positions.astype(jnp.float32)[:, None] * inv_freq[None, :]
    angles = jnp.concatenate([angles, angles], axis=1)
    return (jnp.cos(angles), jnp.sin(angles))


def unrotate(gradient, positions):
    cosine, sine_table = rope_tables(positions, gradient.shape[1])
    half_width = gradient.shape[1] // 2
    turned = jnp.concatenate([-gradient[:, half_width:], gradient[:, :half_width]], axis=1)
    return gradient * cosine - turned * sine_table


def doc_ids(positions, lengths):
    doc_ends = jnp.cumsum(lengths)[:-1]
    return jnp.sum((positions[:, None] >= doc_ends[None, :]).astype(jnp.int32), axis=1)


def seq_to_stored(rows, block_order, device, ctx_size, per_device):
    width = rows.shape[1]
    first_block = device * per_device
    blocks = rows.reshape(per_device, BLOCK, width)
    pieces = []
    for slot_k in range(per_device):
        offset = slot_k * ctx_size // per_device
        slot_at = (device - offset) % ctx_size * per_device + slot_k
        local_index = block_order[slot_at] - first_block
        chosen = lax.dynamic_index_in_dim(blocks, local_index, 0, keepdims=False)
        if slot_k > 0:
            chosen = passed_along(chosen, "ctx", -offset)
        pieces.append(chosen)
    return jnp.concatenate(pieces, axis=0)


def stored_to_seq(rows, block_order, device, ctx_size, per_device):
    width = rows.shape[1]
    first_block = device * per_device
    blocks = rows.reshape(per_device, BLOCK, width)
    pieces = []
    local_ids = []
    for slot_k in range(per_device):
        offset = slot_k * ctx_size // per_device
        piece = blocks[slot_k]
        if slot_k > 0:
            piece = passed_along(piece, "ctx", offset)
        pieces.append(piece)
        sender_slot = (device - offset) % ctx_size * per_device + slot_k
        local_ids.append(block_order[sender_slot] - first_block)
    stacked = jnp.stack(pieces)
    index_list = jnp.stack(local_ids)
    choose = (jnp.arange(per_device, dtype=jnp.int32)[:, None] == index_list[None, :]).astype(
        rows.dtype
    )
    placed = jnp.einsum("pk,kbw->pbw", choose, stacked, preferred_element_type=jnp.float32)
    return placed.astype(rows.dtype).reshape(-1, width)


def contract_rows(left_rows, right_rows):
    return lax.dot_general(
        left_rows, right_rows, (((0,), (0,)), ((), ())), preferred_element_type=jnp.float32
    )


def contract_cols(left_rows, right_rows):
    return lax.dot_general(
        left_rows, right_rows, (((1,), (1,)), ((), ())), preferred_element_type=jnp.float32
    )


def block_scores(query_rows, key_rows, query_pos, query_doc, key_pos, key_doc, score_scale):
    scores = contract_cols(query_rows, key_rows) * score_scale
    visible = (query_doc[:, None] == key_doc[None, :]) & (key_pos[None, :] <= query_pos[:, None])
    return (scores, visible)


def body(grad_in, query, keyval, w_qkv, w_out, doc_lengths, order):
    section_grad_in = grad_in[0]
    stored_query = query[0]
    stored_keyval = keyval[0]
    in_weight = w_qkv[0]
    out_weight = w_out[0]
    lengths = doc_lengths[0]
    block_order = order[0]
    ctx_size = lax.axis_size("ctx")
    device = lax.axis_index("ctx")
    local_rows = section_grad_in.shape[0]
    head_dim = stored_keyval.shape[1] // 2
    group = stored_query.shape[1] // head_dim
    per_device = local_rows // BLOCK
    block_count = block_order.shape[0]
    seq_len = local_rows * ctx_size
    first_row = device * local_rows
    score_scale = 1.0 / math.sqrt(head_dim)
    key_block = math.gcd(seq_len, 512)
    key_steps = seq_len // key_block
    within = jnp.arange(BLOCK, dtype=jnp.int32)
    out_grad = jnp.dot(
        section_grad_in,
        lax.all_gather(out_weight, "ctx", axis=0, tiled=True),
        preferred_element_type=jnp.float32,
    ).astype(jnp.bfloat16)
    local_out_grad = seq_to_stored(out_grad, block_order, device, ctx_size, per_device)
    query_positions = (block_order[:, None] * BLOCK + within[None, :]).reshape(-1)
    gathered = lax.all_gather(stored_keyval, "ctx", axis=0, tiled=True)
    slot_ids = jnp.arange(block_count, dtype=jnp.int32)
    inverse = jnp.sum(
        jnp.where(block_order[None, :] == slot_ids[:, None], slot_ids[None, :], 0), axis=1
    )
    all_keyval = gathered.reshape(block_count, BLOCK, 2 * head_dim)[inverse].reshape(
        seq_len, 2 * head_dim
    )
    key_positions = jnp.arange(seq_len, dtype=jnp.int32)
    key_docs = doc_ids(key_positions, lengths)
    query_pos = lax.dynamic_slice_in_dim(query_positions, first_row, local_rows)
    query_doc = doc_ids(query_pos, lengths)
    flat_rows = local_rows * group
    flat_query = stored_query.reshape(flat_rows, head_dim)
    flat_grad = local_out_grad.reshape(flat_rows, head_dim)
    flat_pos = jnp.repeat(query_pos, group)
    flat_doc = jnp.repeat(query_doc, group)
    key_blocks = (
        all_keyval.reshape(key_steps, key_block, 2 * head_dim),
        key_positions.reshape(key_steps, key_block),
        key_docs.reshape(key_steps, key_block),
    )

    def running_total(carried, current):
        row_top, row_total, weighted = carried
        pair_rows, key_pos, key_doc = current
        scores, visible = block_scores(
            flat_query, pair_rows[:, :head_dim], flat_pos, flat_doc, key_pos, key_doc, score_scale
        )
        new_top = jnp.maximum(row_top, jnp.max(jnp.where(visible, scores, MASKED), axis=1))
        rescale = jnp.exp(row_top - new_top)
        weights = jnp.where(visible, jnp.exp(scores - new_top[:, None]), 0.0)
        row_total = row_total * rescale + jnp.sum(weights, axis=1)
        value_wide = pair_rows[:, head_dim:].astype(jnp.float32)
        weighted = weighted * rescale[:, None] + jnp.dot(
            weights, value_wide, precision=lax.Precision.HIGHEST
        )
        return ((new_top, row_total, weighted), None)

    start_top = jnp.full((flat_rows,), MASKED, jnp.float32)
    start_carry = (
        start_top,
        jnp.zeros((flat_rows,), jnp.float32),
        jnp.zeros((flat_rows, head_dim), jnp.float32),
    )
    (row_top, row_total, weighted), unused = lax.scan(running_total, start_carry, key_blocks)
    log_total = row_top + jnp.log(row_total)
    attn_out = weighted / row_total[:, None]
    row_delta = jnp.sum(flat_grad.astype(jnp.float32) * attn_out, axis=1)

    def grad_step(summed, current):
        pair_rows, key_pos, key_doc = current
        scores, visible = block_scores(
            flat_query, pair_rows[:, :head_dim], flat_pos, flat_doc, key_pos, key_doc, score_scale
        )
        attn_prob = jnp.where(visible, jnp.exp(scores - log_total[:, None]), 0.0)
        prob_grad = contract_cols(flat_grad, pair_rows[:, head_dim:])
        score_grad = (score_scale * attn_prob * (prob_grad - row_delta[:, None])).astype(
            jnp.bfloat16
        )
        summed = summed + jnp.dot(
            score_grad, pair_rows[:, :head_dim], preferred_element_type=jnp.float32
        )
        key_term = contract_rows(score_grad, flat_query)
        value_term = contract_rows(attn_prob.astype(jnp.bfloat16), flat_grad)
        return (summed, jnp.concatenate([key_term, value_term], axis=1))

    query_grad_rot, key_terms = lax.scan(
        grad_step, jnp.zeros((flat_rows, head_dim), jnp.float32), key_blocks
    )
    own_positions = first_row + jnp.arange(local_rows, dtype=jnp.int32)
    keyval_grad = lax.psum_scatter(
        key_terms.reshape(seq_len, 2 * head_dim).astype(jnp.bfloat16),
        "ctx",
        scatter_dimension=0,
        tiled=True,
    ).astype(jnp.float32)
    query_grad = (
        unrotate(query_grad_rot, flat_pos)
        .reshape(local_rows, group * head_dim)
        .astype(jnp.bfloat16)
    )
    query_grad = stored_to_seq(query_grad, block_order, device, ctx_size, per_device)
    key_grad = unrotate(keyval_grad[:, :head_dim], own_positions).astype(jnp.bfloat16)
    value_grad = keyval_grad[:, head_dim:].astype(jnp.bfloat16)
    qkv_grad = jnp.concatenate([query_grad, key_grad, value_grad], axis=1)
    projected = contract_cols(qkv_grad, lax.all_gather(in_weight, "ctx", axis=0, tiled=True))
    section_grad = (section_grad_in.astype(jnp.float32) + projected).astype(jnp.bfloat16)
    passed = passed_along_2(section_grad, "pipe", -1)
    return passed[None]


def solution(mesh):
    return jax.shard_map(
        body,
        mesh=mesh,
        in_specs=(
            P("pipe", "ctx", None),
            P("pipe", "ctx", None),
            P("pipe", "ctx", None),
            P("pipe", "ctx", None),
            P("pipe", "ctx", None),
            P("pipe", None),
            P("pipe", None),
        ),
        out_specs=P("pipe", "ctx", None),
        check_vma=False,
    )
```

profile of v0, /device:TPU:1, one launch (start us, length us, event | category | flops | bytes accessed | tf_op | source)
XLA Modules:
  0.0 424.1 jit_solution(3476864368131219313)
XLA Ops:
  8.1 1.3 constant_dynamic-slice_fusion.5
  10.7 0.8 reduce-window.4
  11.6 1.1 reshape_squeeze.3
  14.5 42.2 %all-gather.7.cloned.1.call-done = bf16[1,4096,256]{2,1,0:T(8,128)(2,1)} async-done(((bf16[1,256,256]{2,1,0:T(8,128)(2,1)}), bf16[1,4096,256]{2,1,0:T(8,128)(2,1)}) %all-gather.7.cloned.1.call-update) | async-done | bytes 2097168 | tf_op jit(solution)/shard_map/all_gather | solution.py:129
  56.7 3.6 gather_fusion
  60.3 51.0 %while.28 = (s32[]{:T(128)}, f32[1024]{0:T(1024)S(1)}, f32[1024]{0:T(1024)S(1)}, f32[1024,128]{1,0:T(8,128)}, s32[8,512]{1,0:T(8,128)S(1)}, /*index=5*/s32[8,512...) while((s32[]{:T(128)}, f32[1024]{0:T(1024)S(1)}, ...), condition=%wide.region_7.8_spmd.clone, body=%wide.region_4.7_spmd.clone.sunk | while | flops 949883904 | bytes 12720321 | solution.py:174
  60.3 1.0 dynamic-slice_bitcast_fusion.6
  63.4 2.4 convolution_add_fusion.4
  65.9 0.8 copy-done.1
  66.7 1.0 dynamic-slice_bitcast_fusion.6
  69.8 2.4 convolution_add_fusion.4
  73.1 1.0 dynamic-slice_bitcast_fusion.6
  76.2 2.4 convolution_add_fusion.4
  79.5 1.0 dynamic-slice_bitcast_fusion.6
  82.6 2.4 convolution_add_fusion.4
  85.8 1.0 dynamic-slice_bitcast_fusion.6
  88.9 2.4 convolution_add_fusion.4
  92.2 1.1 dynamic-slice_bitcast_fusion.6
  95.3 2.4 convolution_add_fusion.4
  98.6 1.0 dynamic-slice_bitcast_fusion.6
  101.7 2.4 convolution_add_fusion.4
  104.9 1.0 dynamic-slice_bitcast_fusion.6
  108.0 2.4 convolution_add_fusion.4
  111.3 18.4 %all-gather.9.cloned.1.call-done = bf16[1,8192,512]{2,1,0:T(8,128)(2,1)} async-done(((bf16[1,512,512]{2,1,0:T(8,128)(2,1)}), bf16[1,8192,512]{2,1,0:T(8,128)(2,1)}) %all-gather.9.cloned.1.call-update) | async-done | bytes 8388624 | tf_op jit(solution)/shard_map/all_gather | solution.py:124
  129.7 7.0 %fusion.43 = bf16[256,512]{1,0:T(8,128)(2,1)S(1)} fusion(bf16[1,8192,512]{2,1,0:T(8,128)(2,1)} %all-gather.9.cloned.1.call-done, bf16[1,256,8192]{2,1,0:T(8,128)(2,1)} %param.11), kind=kOutput, calls=%fused_computation.55 | convolution fusion | flops 2147614720 | bytes 12845056 | tf_op jit(solution)/shard_map/dot_general | solution.py:122
  136.7 2.8 collective-permute-start
  139.5 3.2 collective-permute-done
  143.3 41.0 %while.29 = (s32[]{:T(128)}, f32[1024,128]{1,0:T(8,128)S(1)}, bf16[8,512,256]{2,1,0:T(8,128)(2,1)}, s32[8,512]{1,0:T(8,128)S(1)}, s32[8,512]{1,0:T(8,128)S(1)}, ...) while((s32[]{:T(128)}, f32[1024,128]{1,0:T(8,128)S(1)}, ...), condition=%wide.region_10.11_spmd.clone, body=%wide.region_9.10_spmd.clone.sunk | while | flops 677642240 | bytes 14342807 | solution.py:196
  143.3 1.0 dynamic-slice_bitcast_fusion.7
  148.4 1.0 dynamic-slice_bitcast_fusion.7
  153.5 1.0 dynamic-slice_bitcast_fusion.7
  158.7 1.0 dynamic-slice_bitcast_fusion.7
  163.8 1.0 dynamic-slice_bitcast_fusion.7
  168.9 1.0 dynamic-slice_bitcast_fusion.7
  174.0 1.0 dynamic-slice_bitcast_fusion.7
  179.2 1.0 dynamic-slice_bitcast_fusion.7
  185.6 2.4 fusion.49
  188.1 2.9 collective-permute-start.1
  191.2 2.4 collective-permute-done.1
  194.6 63.0 %reduce-scatter.2.cloned.1.call-done = bf16[256,256]{1,0:T(8,128)(2,1)} async-done(((bf16[4096,256]{1,0:T(8,128)(2,1)}), bf16[256,256]{1,0:T(8,128)(2,1)}) %reduce-scatter.2.cloned.1.call-update) | async-done | bytes 131088 | tf_op jit(solution)/shard_map/reduce_scatter | solution.py:200
  257.6 0.9 convert_element_type.75
  258.5 0.9 slice.79
  259.4 0.8 slice.80
  260.9 89.8 %all-gather.11.cloned.1.call-done = bf16[1,8192,768]{2,1,0:T(8,128)(2,1)} async-done(((bf16[1,512,768]{2,1,0:T(8,128)(2,1)}), bf16[1,8192,768]{2,1,0:T(8,128)(2,1)}) %all-gather.11.cloned.1.call-update) | async-done | bytes 12582928 | tf_op jit(solution)/shard_map/all_gather | solution.py:215
  350.7 14.8 %fusion.37 = bf16[256,8192]{1,0:T(8,128)(2,1)} fusion(bf16[1,8192,768]{2,1,0:T(8,128)(2,1)} %all-gather.11.cloned.1.call-done, bf16[1,256,8192]{2,1,0:T(8,128)(2,1)} %param.11, bf16[256,128]{1,0:T(8,128)(2,1)S(1)} %slice.80, bf16[256,128]{1,0:T(8,128)(2,1)S(1)} %fusion.57, bf16[256,512]{1,0:T(8,128)(2,1)S(1)} %bitcast.123), kind=kOutput, calls=%fused_computation.50 | convolution fusion | flops 3228696576 | bytes 21364736 | tf_op jit(solution)/shard_map/dot_general | solution.py:90
  365.5 2.6 collective-permute-start.2
  368.1 47.5 %collective-permute-done.2 = bf16[256,8192]{1,0:T(8,128)(2,1)S(1)} collective-permute-done((bf16[256,8192]{1,0:T(8,128)(2,1)}, bf16[256,8192]{1,0:T(8,128)(2,1)S(1)}, u32[]{:S(2)}, u32[]{:S(2)}) %collective-permute-start.2) | collective-permute-done | bytes 4194336 | tf_op jit(solution)/shard_map/ppermute | solution.py:21
  415.6 2.0 copy.44
  (262 shorter events, 61.7 us)
Async XLA Ops:
  6.5 50.2 %all-gather.7.cloned.1.call-start = ((), (), s32[]{:S(2)}) async-start(), calls=%async_computation.2 | async-start | bytes 2228224 | tf_op jit(solution)/shard_map/all_gather | solution.py:129
  7.3 122.5 %all-gather.9.cloned.1.call-start = ((), (), s32[]{:S(2)}) async-start(), calls=%async_computation.3 | async-start | bytes 8912896 | tf_op jit(solution)/shard_map/all_gather | solution.py:124
  8.0 249.6 %reduce-scatter.2.cloned.1.call-start = ((), (), s32[]{:S(2)}) async-start(), calls=%async_computation.1 | async-start | bytes 2228224 | tf_op jit(solution)/shard_map/reduce_scatter | solution.py:200
  62.4 1.0 copy-start
  65.9 0.8 copy-start.1
  68.8 1.1 copy-start
  72.3 0.8 copy-start.1
  75.1 1.1 copy-start
  78.6 0.8 copy-start.1
  81.5 1.0 copy-start
  85.0 0.8 copy-start.1
  87.9 1.0 copy-start
  91.3 0.8 copy-start.1
  94.3 1.0 copy-start
  97.8 0.8 copy-start.1
  100.6 1.0 copy-start
  104.1 0.8 copy-start.1
  107.0 1.0 copy-start
  110.5 0.8 copy-start.1
  111.3 31.6 %copy-start.2 = (f32[1024,128]{1,0:T(8,128)S(1)}, f32[1024,128]{1,0:T(8,128)}, u32[]{:S(2)}) copy-start(f32[1024,128]{1,0:T(8,128)} %get-tuple-element.124) | copy-start | bytes 1572868
  136.7 5.9 %collective-permute-start = (bf16[128,512]{1,0:T(8,128)(2,1)S(1)}, bf16[128,512]{1,0:T(8,128)(2,1)S(1)}, u32[]{:S(2)}, u32[]{:S(2)}) collective-permute-start(bf16[128,512]{1,0:T(8,128)(2,1)S(1)} %get-tuple-element.270), channel_id=1, source_target_pairs={{0,8},{1,9},{2,10},{3,11},{4,12},{5,13},{6,14},{7,15},{8,0},{9,1},... | collective-permute-start | bytes 393224 | tf_op jit(solution)/shard_map/ppermute | solution.py:15
  184.3 166.3 %all-gather.11.cloned.1.call-start = ((), (), s32[]{:S(2)}) async-start(), calls=%async_computation.4 | async-start | bytes 13369344 | tf_op jit(solution)/shard_map/all_gather | solution.py:215
  188.1 5.6 %collective-permute-start.1 = (bf16[128,512]{1,0:T(8,128)(2,1)S(1)}, bf16[128,512]{1,0:T(8,128)(2,1)S(1)}, u32[]{:S(2)}, u32[]{:S(2)}) collective-permute-start(bf16[128,512]{1,0:T(8,128)(2,1)S(1)} %slice.59), channel_id=1, source_target_pairs={{0,8},{1,9},{2,10},{3,11},{4,12},{5,13},{6,14},{7,15},{8,0},{9,1},... | collective-permute-start | bytes 393224 | tf_op jit(solution)/shard_map/ppermute | solution.py:15
  365.5 50.1 %collective-permute-start.2 = (bf16[256,8192]{1,0:T(8,128)(2,1)}, bf16[256,8192]{1,0:T(8,128)(2,1)S(1)}, u32[]{:S(2)}, u32[]{:S(2)}) collective-permute-start(bf16[256,8192]{1,0:T(8,128)(2,1)} %fusion.37), channel_id=1, source_target_pairs={{16,0},{32,16},{48,32},{64,48},{80,64},{96,80},{112,96},{17,1},{33... | collective-permute-start | bytes 12582920 | tf_op jit(solution)/shard_map/ppermute | solution.py:21
Sparse Core Ops, SparseCore 0:
  9.5 47.1 all-gather.6
  58.8 70.8 all-gather.8
  184.4 73.1 reduce-scatter.1
  259.8 90.8 all-gather.10
where the time goes:
time: 425 us; the launch traced here: 424 us
  waiting for transfers between devices  269 us (63%)
  matrix products  68.8 us (16%)
  local copies, waits for them, and re-layouts  49.3 us (12%)
  between operations  14.6 us (3%)
  other arithmetic  13 us (3%)
  starting transfers between devices  8.38 us (2%)
    all_gather x1, waiting for transfers between devices, body(): lax.all_gather(in_weight, 'ctx', axis=0, tiled=True)  89.8 us
    reduce_scatter x1, waiting for transfers between devices, body(): lax.psum_scatter(key_terms.reshape(seq_len, 2 * head_dim).astype(jnp.bflo...  63 us
    ppermute x1, waiting for transfers between devices, passed_along_2(): return lax.ppermute(value, axis, pairs)  47.5 us
    all_gather x1, waiting for transfers between devices, body(): gathered = lax.all_gather(stored_keyval, 'ctx', axis=0, tiled=True)  42.2 us
    dot_general x25, matrix products, contract_cols(): lax.dot_general(left_rows, right_rows, (((1,), (1,)), ((), ())), preferre...  29.2 us
    dot_general x8, matrix products, running_total(): jnp.dot(weights, value_wide, precision=lax.Precision.HIGHEST)  19.4 us
    all_gather x1, waiting for transfers between devices, body(): lax.all_gather(out_weight, 'ctx', axis=0, tiled=True)  18.4 us
    squeeze x16, local copies, waits for them, and re-layouts, body(): lax.scan(running_total, start_carry, key_blocks)  15.7 us
  transfers between devices with their start and end apart: 7, of which 7 were waited for; matrix products, arithmetic and copies ran while one was open for 13% of the time, Pallas kernels for 0%

commit v1 on v0

--- a/solution.py
+++ b/solution.py
@@ -126,7 +126,10 @@
     ).astype(jnp.bfloat16)
     local_out_grad = seq_to_stored(out_grad, block_order, device, ctx_size, per_device)
     query_positions = (block_order[:, None] * BLOCK + within[None, :]).reshape(-1)
-    gathered = lax.all_gather(stored_keyval, "ctx", axis=0, tiled=True)
+    devices = lax.axis_size("ctx")
+    parts = jnp.stack([stored_keyval for _ in range(devices)])
+    parts = lax.all_to_all(parts, "ctx", split_axis=0, concat_axis=0)
+    gathered = jnp.concatenate(parts, axis=0)
     slot_ids = jnp.arange(block_count, dtype=jnp.int32)
     inverse = jnp.sum(
         jnp.where(block_order[None, :] == slot_ids[:, None], slot_ids[None, :], 0), axis=1

time: 425 us -> 403 us (0.948)
  waiting for transfers between devices: 269 us -> 246 us
    all_gather x1 -> x0, waiting for transfers between devices: 42.2 us -> none  [body(): gathered = lax.all_gather(stored_keyval, 'ctx', axis=0, tiled=True)]
    all_to_all x0 -> x1, waiting for transfers between devices: none -> 35.5 us  [body(): parts = lax.all_to_all(parts, 'ctx', split_axis=0, concat_axis=0)]
    all_gather x1, waiting for transfers between devices: 18.4 us -> 0.01 us  [body(): lax.all_gather(out_weight, 'ctx', axis=0, tiled=True)]
    all_to_all x0 -> x1, starting transfers between devices: none -> 7.72 us  [body(): parts = lax.all_to_all(parts, 'ctx', split_axis=0, concat_axis=0)]
    ppermute x2, starting transfers between devices: 5.69 us -> 0.92 us  [passed_along(): return lax.ppermute(value, axis, pairs)]
  transfers between devices with their start and end apart: 7 -> 7, of which waited for: 7 -> 6; matrix products, arithmetic and copies ran while one was open for 13% -> 13% of each run, Pallas kernels for 0% -> 0%
where the time goes in v1:
time: 403 us; the launch traced here: 402 us
  waiting for transfers between devices  246 us (61%)
  matrix products  68.4 us (17%)
  local copies, waits for them, and re-layouts  48.6 us (12%)
  between operations  14.8 us (4%)
  starting transfers between devices  11.3 us (3%)
  other arithmetic  11 us (3%)
    all_gather x1, waiting for transfers between devices, body(): lax.all_gather(in_weight, 'ctx', axis=0, tiled=True)  90 us
    reduce_scatter x1, waiting for transfers between devices, body(): lax.psum_scatter(key_terms.reshape(seq_len, 2 * head_dim).astype(jnp.bflo...  62.1 us
    ppermute x1, waiting for transfers between devices, passed_along_2(): return lax.ppermute(value, axis, pairs)  47.5 us
    all_to_all x1, waiting for transfers between devices, body(): parts = lax.all_to_all(parts, 'ctx', split_axis=0, concat_axis=0)  35.5 us
    dot_general x25, matrix products, contract_cols(): lax.dot_general(left_rows, right_rows, (((1,), (1,)), ((), ())), preferre...  29.1 us
    dot_general x8, matrix products, running_total(): jnp.dot(weights, value_wide, precision=lax.Precision.HIGHEST)  19.2 us
    squeeze x16, local copies, waits for them, and re-layouts, body(): lax.scan(running_total, start_carry, key_blocks)  15.6 us
    ppermute x2, waiting for transfers between devices, passed_along(): return lax.ppermute(value, axis, pairs)  9.82 us
  transfers between devices with their start and end apart: 7, of which 6 were waited for; matrix products, arithmetic and copies ran while one was open for 13% of the time, Pallas kernels for 0%

profile of v1, /device:TPU:1, one launch (start us, length us, event | category | flops | bytes accessed | tf_op | source)
XLA Modules:
  0.0 402.0 jit_solution(5406074661522767499)
XLA Ops:
  7.3 2.5 stack.21
  9.7 7.7 %all-to-all-start = ((bf16[16,256,256]{2,1,0:T(8,128)(2,1)}), bf16[16,256,256]{2,1,0:T(8,128)(2,1)S(1)}, u32[]{:S(2)}, u32[]{:S(2)}) async-start(bf16[16,256,256]{2,1,0:T(8,128)(2,1)} %stack.21), calls=%async_computation | async-start | bytes 4194304 | tf_op jit(solution)/shard_map/all_to_all | solution.py:131
  20.5 35.5 %all-to-all-done = bf16[16,256,256]{2,1,0:T(8,128)(2,1)S(1)} async-done(((bf16[16,256,256]{2,1,0:T(8,128)(2,1)}), bf16[16,256,256]{2,1,0:T(8,128)(2,1)S(1)}, u32[]{:S(2)}, u32[]{:S(2)}) %all-to-all-start) | async-done | bytes 2097184 | tf_op jit(solution)/shard_map/all_to_all | solution.py:131
  56.1 2.0 gather_fusion
  58.1 50.7 %while.28 = (s32[]{:T(128)}, f32[1024]{0:T(1024)S(1)}, f32[1024]{0:T(1024)S(1)}, f32[1024,128]{1,0:T(8,128)}, s32[8,512]{1,0:T(8,128)S(1)}, /*index=5*/s32[8,512...) while((s32[]{:T(128)}, f32[1024]{0:T(1024)S(1)}, ...), condition=%wide.region_7.8_spmd.clone, body=%wide.region_4.7_spmd.clone.sunk | while | flops 949883904 | bytes 12720321 | solution.py:177
  58.1 1.0 dynamic-slice_bitcast_fusion.6
  61.2 2.4 convolution_add_fusion.4
  64.4 1.0 dynamic-slice_bitcast_fusion.6
  67.5 2.4 convolution_add_fusion.4
  70.8 1.0 dynamic-slice_bitcast_fusion.6
  73.9 2.4 convolution_add_fusion.4
  76.3 0.8 copy-done.1
  77.1 1.0 dynamic-slice_bitcast_fusion.6
  80.2 2.4 convolution_add_fusion.4
  82.6 0.8 copy-done.1
  83.4 1.0 dynamic-slice_bitcast_fusion.6
  86.5 2.4 convolution_add_fusion.4
  89.0 0.8 copy-done.1
  89.8 1.0 dynamic-slice_bitcast_fusion.6
  92.9 2.4 convolution_add_fusion.4
  95.3 0.8 copy-done.1
  96.1 1.0 dynamic-slice_bitcast_fusion.6
  99.2 2.4 convolution_add_fusion.4
  101.6 0.8 copy-done.1
  102.4 1.0 dynamic-slice_bitcast_fusion.6
  105.5 2.4 convolution_add_fusion.4
  108.8 7.0 %fusion.43 = bf16[256,512]{1,0:T(8,128)(2,1)S(1)} fusion(bf16[1,8192,512]{2,1,0:T(8,128)(2,1)} %all-gather.5.cloned.1.call-done, bf16[1,256,8192]{2,1,0:T(8,128)(2,1)} %param.11), kind=kOutput, calls=%fused_computation.55 | convolution fusion | flops 2147614720 | bytes 12845056 | tf_op jit(solution)/shard_map/dot_general | solution.py:122
  116.2 5.0 %collective-permute-done = bf16[128,512]{1,0:T(8,128)(2,1)S(1)} collective-permute-done((bf16[128,512]{1,0:T(8,128)(2,1)S(1)}, bf16[128,512]{1,0:T(8,128)(2,1)S(1)}, u32[]{:S(2)}, u32[]{:S(2)}) %collective-permute-start) | collective-permute-done | bytes 131104 | tf_op jit(solution)/shard_map/ppermute | solution.py:15
  121.8 40.8 %while.29 = (s32[]{:T(128)}, f32[1024,128]{1,0:T(8,128)S(1)}, bf16[8,512,256]{2,1,0:T(8,128)(2,1)}, s32[8,512]{1,0:T(8,128)S(1)}, s32[8,512]{1,0:T(8,128)S(1)}, ...) while((s32[]{:T(128)}, f32[1024,128]{1,0:T(8,128)S(1)}, ...), condition=%wide.region_10.11_spmd.clone, body=%wide.region_9.10_spmd.clone.sunk | while | flops 677642240 | bytes 14342807 | solution.py:199
  121.8 1.0 dynamic-slice_bitcast_fusion.7
  126.9 1.0 dynamic-slice_bitcast_fusion.7
  132.0 1.0 dynamic-slice_bitcast_fusion.7
  137.1 1.0 dynamic-slice_bitcast_fusion.7
  142.2 1.0 dynamic-slice_bitcast_fusion.7
  147.3 1.0 dynamic-slice_bitcast_fusion.7
  152.4 1.0 dynamic-slice_bitcast_fusion.7
  157.5 1.0 dynamic-slice_bitcast_fusion.7
  164.0 2.4 fusion.49
  167.3 4.8 %collective-permute-done.1 = bf16[128,512]{1,0:T(8,128)(2,1)S(1)} collective-permute-done((bf16[128,512]{1,0:T(8,128)(2,1)S(1)}, bf16[128,512]{1,0:T(8,128)(2,1)S(1)}, u32[]{:S(2)}, u32[]{:S(2)}) %collective-permute-start.1) | collective-permute-done | bytes 131104 | tf_op jit(solution)/shard_map/ppermute | solution.py:15
  173.1 62.1 %reduce-scatter.2.cloned.1.call-done = bf16[256,256]{1,0:T(8,128)(2,1)} async-done(((bf16[4096,256]{1,0:T(8,128)(2,1)}), bf16[256,256]{1,0:T(8,128)(2,1)}) %reduce-scatter.2.cloned.1.call-update) | async-done | bytes 131088 | tf_op jit(solution)/shard_map/reduce_scatter | solution.py:203
  235.2 0.9 convert_element_type.75
  236.1 0.9 slice.79
  237.0 0.8 slice.80
  238.5 90.0 %all-gather.7.cloned.1.call-done = bf16[1,8192,768]{2,1,0:T(8,128)(2,1)} async-done(((bf16[1,512,768]{2,1,0:T(8,128)(2,1)}), bf16[1,8192,768]{2,1,0:T(8,128)(2,1)}) %all-gather.7.cloned.1.call-update) | async-done | bytes 12582928 | tf_op jit(solution)/shard_map/all_gather | solution.py:218
  328.5 14.8 %fusion.37 = bf16[256,8192]{1,0:T(8,128)(2,1)} fusion(bf16[1,8192,768]{2,1,0:T(8,128)(2,1)} %all-gather.7.cloned.1.call-done, bf16[1,256,8192]{2,1,0:T(8,128)(2,1)} %param.11, bf16[256,128]{1,0:T(8,128)(2,1)S(1)} %slice.80, bf16[256,128]{1,0:T(8,128)(2,1)S(1)} %fusion.57, bf16[256,512]{1,0:T(8,128)(2,1)S(1)} %bitcast.124), kind=kOutput, calls=%fused_computation.50 | convolution fusion | flops 3228696576 | bytes 21364736 | tf_op jit(solution)/shard_map/dot_general | solution.py:90
  343.3 2.6 collective-permute-start.2
  345.9 47.5 %collective-permute-done.2 = bf16[256,8192]{1,0:T(8,128)(2,1)S(1)} collective-permute-done((bf16[256,8192]{1,0:T(8,128)(2,1)}, bf16[256,8192]{1,0:T(8,128)(2,1)S(1)}, u32[]{:S(2)}, u32[]{:S(2)}) %collective-permute-start.2) | collective-permute-done | bytes 4194336 | tf_op jit(solution)/shard_map/ppermute | solution.py:21
  393.4 2.0 copy.44
  (268 shorter events, 58.3 us)
Async XLA Ops:
  6.5 102.2 %all-gather.5.cloned.1.call-start = ((), (), s32[]{:S(2)}) async-start(), calls=%async_computation.3 | async-start | bytes 8912896 | tf_op jit(solution)/shard_map/all_gather | solution.py:124
  9.7 7.8 %copy-start.4 = (s32[1,32]{1,0:T(1,128)S(1)}, s32[1,32]{1,0:T(1,128)}, u32[]{:S(2)}) copy-start(s32[1,32]{1,0:T(1,128)} %param.17) | copy-start | bytes 388
  9.7 9.9 %copy-start.5 = (s32[1,8]{1,0:T(1,128)S(1)}, s32[1,8]{1,0:T(1,128)}, u32[]{:S(2)}) copy-start(s32[1,8]{1,0:T(1,128)} %param.16) | copy-start | bytes 100
  9.7 10.2 %copy-start.3 = (bf16[1,256,512]{2,1,0:T(8,128)(2,1)S(1)}, bf16[1,256,512]{2,1,0:T(8,128)(2,1)}, u32[]{:S(2)}) copy-start(bf16[1,256,512]{2,1,0:T(8,128)(2,1)} %param.12) | copy-start | bytes 786436
  9.7 46.3 %all-to-all-start = ((bf16[16,256,256]{2,1,0:T(8,128)(2,1)}), bf16[16,256,256]{2,1,0:T(8,128)(2,1)S(1)}, u32[]{:S(2)}, u32[]{:S(2)}) async-start(bf16[16,256,256]{2,1,0:T(8,128)(2,1)} %stack.21), calls=%async_computation | async-start | bytes 4194304 | tf_op jit(solution)/shard_map/all_to_all | solution.py:131
  17.4 217.8 %reduce-scatter.2.cloned.1.call-start = ((), (), s32[]{:S(2)}) async-start(), calls=%async_computation.2 | async-start | bytes 2228224 | tf_op jit(solution)/shard_map/reduce_scatter | solution.py:203
  60.2 1.0 copy-start
  63.6 0.8 copy-start.1
  66.5 1.0 copy-start
  69.9 0.8 copy-start.1
  72.8 1.1 copy-start
  76.3 0.8 copy-start.1
  79.2 1.0 copy-start
  82.6 0.8 copy-start.1
  85.5 1.0 copy-start
  88.9 0.8 copy-start.1
  91.8 1.0 copy-start
  95.3 0.8 copy-start.1
  98.2 1.0 copy-start
  101.6 0.8 copy-start.1
  104.5 1.0 copy-start
  107.9 0.8 copy-start.1
  108.8 12.7 %copy-start.2 = (f32[1024,128]{1,0:T(8,128)S(1)}, f32[1024,128]{1,0:T(8,128)}, u32[]{:S(2)}) copy-start(f32[1024,128]{1,0:T(8,128)} %get-tuple-element.124) | copy-start | bytes 1572868
  115.8 5.4 %collective-permute-start = (bf16[128,512]{1,0:T(8,128)(2,1)S(1)}, bf16[128,512]{1,0:T(8,128)(2,1)S(1)}, u32[]{:S(2)}, u32[]{:S(2)}) collective-permute-start(bf16[128,512]{1,0:T(8,128)(2,1)S(1)} %get-tuple-element.270), channel_id=1, source_target_pairs={{0,8},{1,9},{2,10},{3,11},{4,12},{5,13},{6,14},{7,15},{8,0},{9,1},... | collective-permute-start | bytes 393224 | tf_op jit(solution)/shard_map/ppermute | solution.py:15
  162.6 165.8 %all-gather.7.cloned.1.call-start = ((), (), s32[]{:S(2)}) async-start(), calls=%async_computation.4 | async-start | bytes 13369344 | tf_op jit(solution)/shard_map/all_gather | solution.py:218
  166.5 5.6 %collective-permute-start.1 = (bf16[128,512]{1,0:T(8,128)(2,1)S(1)}, bf16[128,512]{1,0:T(8,128)(2,1)S(1)}, u32[]{:S(2)}, u32[]{:S(2)}) collective-permute-start(bf16[128,512]{1,0:T(8,128)(2,1)S(1)} %slice.59), channel_id=1, source_target_pairs={{0,8},{1,9},{2,10},{3,11},{4,12},{5,13},{6,14},{7,15},{8,0},{9,1},... | collective-permute-start | bytes 393224 | tf_op jit(solution)/shard_map/ppermute | solution.py:15
  343.3 50.1 %collective-permute-start.2 = (bf16[256,8192]{1,0:T(8,128)(2,1)}, bf16[256,8192]{1,0:T(8,128)(2,1)S(1)}, u32[]{:S(2)}, u32[]{:S(2)}) collective-permute-start(bf16[256,8192]{1,0:T(8,128)(2,1)} %fusion.37), channel_id=1, source_target_pairs={{16,0},{32,16},{48,32},{64,48},{80,64},{96,80},{112,96},{17,1},{33... | collective-permute-start | bytes 12582920 | tf_op jit(solution)/shard_map/ppermute | solution.py:21
Sparse Core Ops, SparseCore 0:
  9.5 90.3 all-gather.4
  162.8 72.4 reduce-scatter.1
  237.6 90.8 all-gather.6
